TPU v7x, 32 devices: a whole 2x2x4 slice. The times are simulated.
32 devices in a mesh: req: 4 (over y, x), exp: 4 (over z), ffn: 2 (over core).
Axes of the slice: x: 2, y: 2, z: 4, core: 2. Of those that a mesh axis runs over, the one named last changes fastest.
Arguments:
- residual: bfloat16 [2048, 2048], P(('req', 'exp')), may hold values from -5 to 5
- queries: bfloat16 [2048, 4608], P(('req', 'exp'), 'ffn'), may hold values from -30 to 30
- new_latent: bfloat16 [2048, 576], P(('req', 'exp')), may hold values from -6 to 6
- cache_pool: bfloat16 [512, 9216], P(('req', 'exp')), may hold values from -5 to 5
- page_table: int32 [8, 64], replicated, may hold values from 0 to 511, as said below
- cached_len: int32 [8], replicated, may hold values from 0 to 1024
- tenant_start: int32 [8], replicated, may hold values from 0 to 512, as said below
- routes: int32 [2048, 6], P(('req', 'exp')), may hold values from 0 to 31, all different within a row; in each aligned block of 64 rows (0 to 63, 64 to 127, ...) at most 16 rows name the same one
- value_up: bfloat16 [512, 1024], P(None, 'ffn'), may hold values from -0.25 to 0.25
- out_proj: bfloat16 [1024, 2048], P('ffn'), may hold values from -0.1875 to 0.1875
- norm_gain: bfloat16 [2048], replicated, may hold values from 0.099609375 to 1.8984375
- router: bfloat16 [2048, 32], replicated, may hold values from -0.125 to 0.125
- gate_weight: bfloat16 [32, 2048, 1408], P('exp', None, 'ffn'), may hold values from -0.125 to 0.125
- up_weight: bfloat16 [32, 2048, 1408], P('exp', None, 'ffn'), may hold values from -0.125 to 0.125
- down_weight: bfloat16 [32, 1408, 2048], P('exp', 'ffn'), may hold values from -0.15625 to 0.15625
Outputs:
- hidden_out: bfloat16 [2048, 2048], P(('req', 'exp'), 'ffn')
- moe_out: bfloat16 [2048, 2048], P(('req', 'exp'), 'ffn')
Inputs may be any that keep to these rules, and one draw needn't show every extreme that they name: `page_table`: row i lists, in order, the pool pages of request i's cache; the 2 requests of group g = i // 2 use pool pages g * 2 * 64 to (g + 1) * 2 * 64 - 1, each exactly once. tenant_start[i] is at most half of cached_len[i]. `routes`: A row names 6 different experts; in each aligned block of 64 rows at most 16 rows name the same expert.
All inputs are finite; a program needn't handle non-finite values.
Results may differ from a plain program's by a relative error of at most 0.025.
Values may be sent and summed in bfloat16 or wider, within the bound.
No kernel may reach another device: no remote copies, remote signals or barrier semaphores. Data moves between devices by JAX's collectives and lax.ppermute only.
A program may use at most 128 MiB of HBM per device.

v0:
```python
import jax
import jax.numpy as jnp
from jax import lax
from jax.sharding import PartitionSpec as P

LATENT = 512
ROPE_DIM = 64
HEAD_DIM = 128
QKD = 576
EXPERTS = 32
TOP = 6
CAPACITY = 16
REQ_GRP = 2
CMAX = 1024
BLOCK_ROWS = 64
EPSILON = 1e-06
NEG_FILL = -1e30


def local(
    residual,
    queries,
    new_latent,
    cache_pool,
    page_table,
    cached_len,
    tenant_start,
    routes,
    value_up,
    out_proj,
    norm_gain,
    router,
    gate_weight,
    up_weight,
    down_weight,
):
    exp_size = lax.axis_size("exp")
    ffn_size = lax.axis_size("ffn")
    req_index = lax.axis_index("req")
    exp_index = lax.axis_index("exp")
    ffn_index = lax.axis_index("ffn")
    token_rows = residual.shape[0]
    feature_count = residual.shape[1]
    fresh_len = token_rows * exp_size // REQ_GRP
    first_token = (req_index * exp_size + exp_index) * token_rows
    request = first_token // fresh_len
    offset = first_token - request * fresh_len
    pool_pages = cache_pool.shape[0]
    page_width = cache_pool.shape[1]
    latent_pages = token_rows * QKD // page_width
    route_count = token_rows * TOP
    route_pages = -(-route_count // page_width)
    route_rows = jnp.pad(
        routes.reshape(route_count).astype(jnp.bfloat16),
        (0, route_pages * page_width - route_count),
    ).reshape(route_pages, page_width)
    packed_rows = pool_pages + latent_pages + route_pages
    share_rows = -(-packed_rows // ffn_size)
    packed = jnp.concatenate(
        [
            cache_pool,
            new_latent.reshape(latent_pages, page_width),
            route_rows,
            jnp.zeros((share_rows * ffn_size - packed_rows, page_width), jnp.bfloat16),
        ],
        axis=0,
    )
    share = lax.dynamic_slice_in_dim(packed, ffn_index * share_rows, share_rows, 0)
    gathered = lax.all_gather(share, ("exp", "ffn"), axis=0, tiled=False)
    gathered = gathered.reshape(exp_size, ffn_size * share_rows, page_width)
    stride = ffn_size * share_rows
    group_rows = exp_size * token_rows
    routes_all = (
        gathered[:, pool_pages + latent_pages : packed_rows]
        .reshape(exp_size, route_pages * page_width)[:, :route_count]
        .reshape(group_rows, TOP)
        .astype(jnp.int32)
    )
    flat_pages = gathered.reshape(exp_size * stride, page_width)
    pool_base = req_index * exp_size * pool_pages
    page_rows = page_table[request] - pool_base
    cached_rows = page_rows // pool_pages * stride + page_rows % pool_pages
    local_request = request - req_index * REQ_GRP
    fresh_devices = fresh_len // token_rows
    fresh_index = lax.broadcasted_iota(jnp.int32, (fresh_devices, latent_pages), 0)
    fresh_rows = (
        (local_request * fresh_devices + fresh_index) * stride
        + pool_pages
        + lax.broadcasted_iota(jnp.int32, (fresh_devices, latent_pages), 1)
    ).reshape(fresh_devices * latent_pages)
    key_rows = jnp.concatenate([cached_rows, fresh_rows], axis=0)
    all_keys = jnp.take(flat_pages, key_rows, axis=0).reshape(CMAX + fresh_len, QKD)
    heads_here = queries.shape[1] // QKD
    query_heads = queries.reshape(token_rows, heads_here, QKD)
    scale_factor = (HEAD_DIM + ROPE_DIM) ** (-0.5)
    scores = (
        jnp.einsum("thd,kd->thk", query_heads, all_keys, preferred_element_type=jnp.float32)
        * scale_factor
    )
    key_pos = lax.broadcasted_iota(jnp.int32, (1, CMAX + fresh_len), 1)
    tok_pos = offset + lax.broadcasted_iota(jnp.int32, (token_rows, 1), 0)
    cached_ok = (key_pos >= tenant_start[request]) & (key_pos < cached_len[request])
    fresh_ok = (key_pos >= CMAX) & (key_pos - CMAX <= tok_pos)
    visible = cached_ok | fresh_ok
    scores = jnp.where(visible[:, None, :], scores, NEG_FILL)
    top_score = jnp.max(scores, axis=2, keepdims=True)
    weights = jnp.exp(scores - top_score)
    attn_probs = (weights / jnp.sum(weights, axis=2, keepdims=True)).astype(jnp.bfloat16)
    latent_out = jnp.einsum(
        "thk,kl->thl", attn_probs, all_keys[:, :LATENT], preferred_element_type=jnp.float32
    ).astype(jnp.bfloat16)
    value_heads = value_up.reshape(LATENT, heads_here, HEAD_DIM)
    head_out = jnp.einsum(
        "thl,lhd->thd", latent_out, value_heads, preferred_element_type=jnp.float32
    )
    head_out = head_out.astype(jnp.bfloat16).reshape(token_rows, heads_here * HEAD_DIM)
    partial_value = jnp.dot(head_out, out_proj, preferred_element_type=jnp.float32)
    column_count = feature_count // ffn_size
    attn_cols = lax.psum_scatter(
        partial_value.astype(jnp.bfloat16), "ffn", scatter_dimension=1, tiled=True
    ).astype(jnp.float32)
    residual_cols = lax.dynamic_slice_in_dim(residual, ffn_index * column_count, column_count, 1)
    hidden_out = (residual_cols.astype(jnp.float32) + attn_cols).astype(jnp.bfloat16)
    hidden_wide = hidden_out.astype(jnp.float32)
    square_sum = lax.psum(jnp.sum(hidden_wide * hidden_wide, axis=1, keepdims=True), "ffn")
    mean_square = square_sum / feature_count
    gain_cols = lax.dynamic_slice_in_dim(norm_gain, ffn_index * column_count, column_count, 0)
    normed_cols = (
        hidden_wide * lax.rsqrt(mean_square + EPSILON) * gain_cols.astype(jnp.float32)
    ).astype(jnp.bfloat16)
    normed_half = lax.all_gather(normed_cols, "exp", axis=0, tiled=True)
    normed_all = lax.all_gather(normed_half, "ffn", axis=1, tiled=True)
    expert_ids = lax.broadcasted_iota(jnp.int32, (1, 1, EXPERTS), 2)
    route_hot = routes_all[:, :, None] == expert_ids
    blocks = group_rows // BLOCK_ROWS
    pair_count = BLOCK_ROWS * TOP
    pair_hot = route_hot.reshape(blocks, pair_count, EXPERTS).astype(jnp.bfloat16)
    earlier = (
        lax.broadcasted_iota(jnp.int32, (pair_count, pair_count), 1)
        < lax.broadcasted_iota(jnp.int32, (pair_count, pair_count), 0)
    ).astype(jnp.bfloat16)
    before = jnp.einsum("pq,bqx->bpx", earlier, pair_hot, preferred_element_type=jnp.float32)
    rank = jnp.sum(before * pair_hot.astype(jnp.float32), axis=2).astype(jnp.int32)
    block_base = lax.broadcasted_iota(jnp.int32, (blocks, 1), 0) * CAPACITY
    slot_index = (rank + block_base).reshape(group_rows, TOP)
    slot_count = blocks * CAPACITY
    local_count = gate_weight.shape[0]
    total_slots = local_count * slot_count
    local_expert = routes_all - exp_index * local_count
    is_local = (local_expert >= 0) & (local_expert < local_count)
    target = jnp.where(is_local, local_expert * slot_count + slot_index, -1)
    logits = jnp.dot(normed_all, router, preferred_element_type=jnp.float32)
    chosen = jnp.sum(jnp.where(route_hot, logits[:, None, :], 0.0), axis=2)
    raised = jnp.exp(chosen)
    gate_weights = raised / jnp.sum(raised, axis=1, keepdims=True)
    slot_ids = lax.broadcasted_iota(jnp.int32, (1, 1, total_slots), 2)
    slot_hit = target[:, :, None] == slot_ids
    combine = jnp.any(slot_hit, axis=1).astype(jnp.bfloat16)
    slot_weight = jnp.sum(jnp.where(slot_hit, gate_weights[:, :, None], 0.0), axis=(0, 1))
    dispatch_ids = lax.broadcasted_iota(jnp.int32, (total_slots, 1, 1), 0)
    dispatch = jnp.any(target[None, :, :] == dispatch_ids, axis=2).astype(jnp.bfloat16)
    grouped = jnp.dot(dispatch, normed_all, preferred_element_type=jnp.float32).astype(jnp.bfloat16)
    grouped = grouped.reshape(local_count, slot_count, feature_count)
    gate_part = jnp.einsum("jmd,jdf->jmf", grouped, gate_weight, preferred_element_type=jnp.float32)
    up_part = jnp.einsum("jmd,jdf->jmf", grouped, up_weight, preferred_element_type=jnp.float32)
    active = (jax.nn.silu(gate_part) * up_part).astype(jnp.bfloat16)
    outputs = jnp.einsum("jmf,jfd->jmd", active, down_weight, preferred_element_type=jnp.float32)
    weighted = (outputs.reshape(total_slots, feature_count) * slot_weight[:, None]).astype(
        jnp.bfloat16
    )
    mixture = jnp.dot(combine, weighted, preferred_element_type=jnp.float32).astype(jnp.bfloat16)
    moe_cols = lax.psum_scatter(mixture, "ffn", scatter_dimension=1, tiled=True)
    moe_out = lax.psum_scatter(moe_cols, "exp", scatter_dimension=0, tiled=True)
    return (hidden_out, moe_out)


def solution(mesh):
    in_specs = (
        P(("req", "exp"), None),
        P(("req", "exp"), "ffn"),
        P(("req", "exp"), None),
        P(("req", "exp"), None),
        P(),
        P(),
        P(),
        P(("req", "exp"), None),
        P(None, "ffn"),
        P("ffn", None),
        P(),
        P(),
        P("exp", None, "ffn"),
        P("exp", None, "ffn"),
        P("exp", "ffn", None),
    )
    out_specs = (P(("req", "exp"), "ffn"), P(("req", "exp"), "ffn"))
    return jax.shard_map(local, mesh=mesh, in_specs=in_specs, out_specs=out_specs, check_vma=False)
```

profile of v0, /device:TPU:0, one launch (start us, length us, event | category | flops | bytes accessed | tf_op | source)
XLA Modules:
  0.0 243.3 jit_solution(17411121236919590765)
XLA Ops:
  7.2 1.2 copy.43
  8.5 0.2 reshape.346
  8.7 0.7 convert_element_type.101
  9.4 0.1 copy.44
  9.5 0.2 convert_element_type.102
  9.7 0.1 pad.10.clone
  9.8 0.1 dynamic-slice
  9.8 2.3 fusion.36
  12.3 0.1 iota_add_fusion.1
  12.3 0.1 concatenate.36
  12.4 0.1 add.210
  12.5 1.2 dynamic_slice.19
  13.7 1.2 dynamic_slice.20
  15.0 0.3 copy.45
  15.3 0.7 fusion.40
  16.0 0.1 compare_and_fusion
  16.1 0.1 broadcast_in_dim.80
  16.2 0.1 broadcast_in_dim.81
  16.3 1.3 copy.55
  17.5 0.7 fusion.69
  18.2 0.1 fusion.43
  18.3 1.3 iota_compare_fusion.6
  19.6 1.0 and_or_fusion
  20.7 35.9 %all-gather.10.cloned.1.call-done = bf16[8,21,9216]{2,1,0:T(8,128)(2,1)} async-done(((bf16[1,21,9216]{2,1,0:T(8,128)(2,1)}), bf16[8,21,9216]{2,1,0:T(8,128)(2,1)}) %all-gather.10.cloned.1.call-update) | async-done | bytes 3096592 | tf_op jit(solution)/shard_map/all_gather | solution.py:69
  56.6 4.8 %reshape.369 = bf16[168,9216]{1,0:T(8,128)(2,1)} reshape(bf16[8,21,9216]{2,1,0:T(8,128)(2,1)} %all-gather.10.cloned.1.call-done) | data formatting | bytes 6193152
  61.4 6.3 %gather_fusion = bf16[80,9216]{1,0:T(8,128)(2,1)} fusion(bf16[168,9216]{1,0:T(8,128)(2,1)} %reshape.369, s32[1024]{0:T(1024)S(1)} %pad_clamp_fusion), kind=kCustom, calls=%fused_computation | custom fusion | bytes 2949440 | tf_op jit(solution)/shard_map/jit(_take)/gather | solution.py:92
  67.7 2.7 %broadcast_select_fusion = bf16[80,9216]{1,0:T(8,128)(2,1)} fusion(bf16[80,9216]{1,0:T(8,128)(2,1)} %gather_fusion, pred[80]{0:T(512)(128)(4,1)S(1)} %compare_and_fusion), kind=kLoop, calls=%fused_computation.21 | loop fusion | flops 737280 | bytes 2949200 | tf_op jit(solution)/shard_map/jit(_take)/select_n | solution.py:92
  70.3 3.9 %gather.7 = bf16[1280,576]{1,0:T(8,128)(2,1)} reshape(bf16[80,9216]{1,0:T(8,128)(2,1)} %gather_fusion) | data formatting | bytes 2949120 | tf_op jit(solution)/shard_map/jit(_take)/gather | solution.py:92
  74.2 3.9 %select_n.117 = bf16[1280,576]{1,0:T(8,128)(2,1)} reshape(bf16[80,9216]{1,0:T(8,128)(2,1)} %broadcast_select_fusion) | data formatting | bytes 2949120 | tf_op jit(solution)/shard_map/jit(_take)/select_n | solution.py:92
  78.1 2.6 %fusion.6 = f32[128,4,1280]{0,2,1:T(8,128)S(1)} fusion(bf16[128,4,576]{0,2,1:T(8,128)(2,1)S(1)} %bitcast.75, bf16[1280,576]{1,0:T(8,128)(2,1)} %select_n.117, pred[128,1280]{0,1:T(8,128)(4,1)S(1)} %and_or_fusion), kind=kOutput, calls=%fused_computation.13 | convolution fusion | flops 756285440 | bytes 4849664 | tf_op jit(solution)/shard_map/thd,kd->thk/dot_general | solution.py:97
  80.8 1.5 copy-done.3
  82.3 0.6 fusion.49
  82.9 4.4 %fusion.23 = bf16[4,128,128]{1,2,0:T(8,128)(2,1)S(1)} fusion(bf16[512,4,128]{0,2,1:T(8,128)(2,1)S(1)} %bitcast.76, bf16[1280,576]{1,0:T(8,128)(2,1)} %gather.7, pred[1280]{0:T(1024)(128)(4,1)S(1)} %broadcast_in_dim.81, f32[128,4]{0,1:T(4,128)S(1)} %fusion.49, f32[128,4,1280]{0,2,1:T(8,128)} %copy-done.3), kind=kOutput, calls=%fused_computation.32 | convolution fusion | flops 741148416 | bytes 7212288 | tf_op jit(solution)/shard_map/thl,lhd->thd/dot_general | solution.py:113
  87.3 1.3 convolution_convert_fusion.2
  88.5 0.2 all-gather.6.cloned.1.call-start
  88.8 6.7 %reduce-scatter.4.cloned.1.call-done = bf16[128,1024]{1,0:T(8,128)(2,1)} async-done(((bf16[128,2048]{1,0:T(8,128)(2,1)}), bf16[128,1024]{1,0:T(8,128)(2,1)}) %reduce-scatter.4.cloned.1.call-update) | async-done | bytes 262160 | tf_op jit(solution)/shard_map/reduce_scatter | solution.py:119
  95.5 1.1 fusion.30
  96.6 2.5 %psum.7 = f32[128,1]{0,1:T(1,128)S(1)} all-reduce(f32[128,1]{0,1:T(1,128)S(1)} %bitcast.79), channel_id=1, replica_groups=mesh['req'=4,'exp'=4,'ffn'=2] {'ffn'}, use_global_device_ids=true, to_apply=%region_7.8 | all-reduce | flops 128 | bytes 1024 | tf_op jit(solution)/shard_map/psum | solution.py:125
  99.1 0.8 fusion.32
  100.0 29.2 %all-gather.6.cloned.1.call-done = bf16[512,1024]{1,0:T(8,128)(2,1)} async-done(((bf16[128,1024]{1,0:T(8,128)(2,1)}), bf16[512,1024]{1,0:T(8,128)(2,1)}) %all-gather.6.cloned.1.call-update) | async-done | bytes 1048592 | tf_op jit(solution)/shard_map/all_gather | solution.py:131
  129.3 0.1 add.217
  129.4 0.1 add.218
  129.4 4.7 %reshape.351 = bf16[4,42,9216]{2,1,0:T(8,128)(2,1)} reshape(bf16[8,21,9216]{2,1,0:T(8,128)(2,1)} %all-gather.10.cloned.1.call-done) | data formatting | bytes 6193152 | tf_op jit(solution)/shard_map/reshape | solution.py:70
  134.1 1.2 slice.15
  135.4 0.2 reshape.355
  135.6 0.1 copy.51
  135.7 0.3 fusion.22
  136.0 0.2 convert_element_type.117
  136.2 0.1 add_select_fusion
  136.4 0.1 copy.49
  136.5 2.3 fusion.2
  138.8 1.4 fusion.1
  140.2 0.6 all-gather.8.cloned.1.call-done
  140.8 2.3 fusion.51
  143.1 0.1 select_reduce_fusion.1
  143.2 1.7 select_reduce_fusion
  145.0 3.9 %convolution_convert_fusion = bf16[1024,2048]{1,0:T(8,128)(2,1)S(1)} fusion(pred[1024,512]{1,0:T(8,128)(4,1)S(1)} %fusion.2, bf16[512,2048]{1,0:T(8,128)(2,1)} %all-gather.8.cloned.1.call-done), kind=kOutput, calls=%fused_computation.9 | convolution fusion | flops 2149580800 | bytes 6815744 | tf_op jit(solution)/shard_map/dot_general | solution.py:162
  148.9 2.0 copy-done.2
  150.9 12.3 %fusion.50 = f32[8,128,704]{1,2,0:T(8,128)} fusion(bf16[8,128,2048]{2,1,0:T(8,128)(2,1)S(1)} %bitcast.73, bf16[8,2048,704]{1,2,0:T(8,128)(2,1)} %param.27), kind=kOutput, calls=%fused_computation.89 | convolution fusion | flops 2952790016 | bytes 30146560 | tf_op jit(solution)/shard_map/jmd,jdf->jmf/dot_general | solution.py:164
  163.2 23.6 %fusion.8 = f32[8,128,2048]{2,1,0:T(8,128)} fusion(bf16[8,704,2048]{2,1,0:T(8,128)(2,1)} %param.29, f32[8,128,704]{1,2,0:T(8,128)} %fusion.50, bf16[8,128,2048]{2,1,0:T(8,128)(2,1)} %bitcast.74, bf16[8,2048,704]{1,2,0:T(8,128)(2,1)} %param.28), kind=kOutput, calls=%fused_computation.19 | convolution fusion | flops 5909905408 | bytes 61603840 | tf_op jit(solution)/shard_map/jmf,jfd->jmd/dot_general | solution.py:167
  186.7 3.9 %fusion.3 = bf16[1024,2048]{1,0:T(8,128)(2,1)S(1)} fusion(f32[8,128,2048]{2,1,0:T(8,128)} %fusion.8, f32[1024]{0:T(1024)S(1)} %select_reduce_fusion), kind=kLoop, calls=%fused_computation.8 | loop fusion | flops 4194304 | bytes 12587008 | tf_op jit(solution)/shard_map/convert_element_type | solution.py:168
  190.6 3.7 %convolution_convert_fusion.1 = bf16[512,2048]{1,0:T(8,128)(2,1)} fusion(pred[512,1024]{1,0:T(8,128)(4,1)S(1)} %fusion.1, bf16[1024,2048]{1,0:T(8,128)(2,1)S(1)} %fusion.3), kind=kOutput, calls=%fused_computation.15 | convolution fusion | flops 2148532224 | bytes 6815744 | tf_op jit(solution)/shard_map/dot_general | solution.py:171
  194.5 10.9 %reduce-scatter.6.cloned.1.call-done = bf16[512,1024]{1,0:T(8,128)(2,1)} async-done(((bf16[512,2048]{1,0:T(8,128)(2,1)}), bf16[512,1024]{1,0:T(8,128)(2,1)}) %reduce-scatter.6.cloned.1.call-update) | async-done | bytes 1048592 | tf_op jit(solution)/shard_map/reduce_scatter | solution.py:172
  205.4 31.1 %reduce-scatter.8.cloned.1.call-done = bf16[128,1024]{1,0:T(8,128)(2,1)} async-done(((bf16[512,1024]{1,0:T(8,128)(2,1)}), bf16[128,1024]{1,0:T(8,128)(2,1)}) %reduce-scatter.8.cloned.1.call-update) | async-done | bytes 262160 | tf_op jit(solution)/shard_map/reduce_scatter | solution.py:173
  (42 shorter events, 0.5 us)
Async XLA Ops:
  7.2 80.1 %copy-start = (bf16[512,2048]{1,0:T(8,128)(2,1)S(1)}, bf16[512,2048]{1,0:T(8,128)(2,1)}, u32[]{:S(2)}) copy-start(bf16[512,2048]{1,0:T(8,128)(2,1)} %param.24) | copy-start | bytes 6291460
  7.2 7.8 %copy-start.5 = (bf16[128,2304]{1,0:T(8,128)(2,1)S(1)}, bf16[128,2304]{1,0:T(8,128)(2,1)}, u32[]{:S(2)}) copy-start(bf16[128,2304]{1,0:T(8,128)(2,1)} %param.16) | copy-start | bytes 1769476
  7.2 49.4 %all-gather.10.cloned.1.call-start = ((), (), s32[]{:S(2)}) async-start(), calls=%async_computation.8 | async-start | bytes 3981312 | tf_op jit(solution)/shard_map/all_gather | solution.py:69
  12.2 83.3 %reduce-scatter.4.cloned.1.call-start = ((), (), s32[]{:S(2)}) async-start(), calls=%async_computation.3 | async-start | bytes 786432 | tf_op jit(solution)/shard_map/reduce_scatter | solution.py:119
  80.8 1.5 copy-start.3
  87.2 1.6 copy-start.8
  87.2 8.3 %copy-start.7 = (bf16[128,2048]{1,0:T(8,128)(2,1)S(1)}, bf16[128,2048]{1,0:T(8,128)(2,1)}, u32[]{:S(2)}) copy-start(bf16[128,2048]{1,0:T(8,128)(2,1)} %param.15) | copy-start | bytes 1572868
  88.5 40.7 %all-gather.6.cloned.1.call-start = ((), (), s32[]{:S(2)}) async-start(), calls=%async_computation.4 | async-start | bytes 1310720 | tf_op jit(solution)/shard_map/all_gather | solution.py:131
  96.6 37.5 %copy-start.4 = (bf16[128,1024]{1,0:T(8,128)(2,1)}, bf16[128,1024]{1,0:T(8,128)(2,1)S(1)}, u32[]{:S(2)}) copy-start(bf16[128,1024]{1,0:T(8,128)(2,1)S(1)} %get-tuple-element.3) | copy-start | bytes 786436
  100.0 40.8 %all-gather.8.cloned.1.call-start = ((), (), s32[]{:S(2)}) async-start(), calls=%async_computation.5 | async-start | bytes 3145728 | tf_op jit(solution)/shard_map/all_gather | solution.py:132
  129.2 76.1 %reduce-scatter.6.cloned.1.call-start = ((), (), s32[]{:S(2)}) async-start(), calls=%async_computation.6 | async-start | bytes 3145728 | tf_op jit(solution)/shard_map/reduce_scatter | solution.py:172
  134.1 6.7 %copy-start.6 = (bf16[2048,32]{0,1:T(8,128)(2,1)S(1)}, bf16[2048,32]{0,1:T(8,128)(2,1)}, u32[]{:S(2)}) copy-start(bf16[2048,32]{0,1:T(8,128)(2,1)} %param.26) | copy-start | bytes 393220
  148.9 2.0 copy-start.2
  190.6 45.8 %copy-start.1 = (bf16[512,2048]{1,0:T(8,128)(2,1)S(1)}, bf16[512,2048]{1,0:T(8,128)(2,1)}, u32[]{:S(2)}) copy-start(bf16[512,2048]{1,0:T(8,128)(2,1)} %param.24) | copy-start | bytes 6291460
  194.4 42.0 %reduce-scatter.8.cloned.1.call-start = ((), (), s32[]{:S(2)}) async-start(), calls=%async_computation.7 | async-start | bytes 1310720 | tf_op jit(solution)/shard_map/reduce_scatter | solution.py:173
Sparse Core Ops, SparseCore 0:
  12.3 44.2 all-gather.9
  88.7 6.7 reduce-scatter.3
  100.1 29.0 all-gather.5
  130.7 10.0 all-gather.7
  194.5 10.7 reduce-scatter.5
  208.1 28.3 reduce-scatter.7
where the time goes:
time: 244 us; the launch traced here: 243 us
  waiting for transfers between devices  114 us (47%)
  matrix products  54.4 us (22%)
  local copies, waits for them, and re-layouts  35.3 us (14%)
  other arithmetic  21.8 us (9%)
  between operations  14.5 us (6%)
  blocking collectives  2.47 us (1%)
    all_gather x1, waiting for transfers between devices, local(): gathered = lax.all_gather(share, ('exp', 'ffn'), axis=0, tiled=False)  35.9 us
    reduce_scatter x1, waiting for transfers between devices, local(): moe_out = lax.psum_scatter(moe_cols, 'exp', scatter_dimension=0, tiled=True)  31.1 us
    all_gather x1, waiting for transfers between devices, local(): normed_half = lax.all_gather(normed_cols, 'exp', axis=0, tiled=True)  29.2 us
    dot_general x1, matrix products, local(): jnp.einsum('jmf,jfd->jmd', active, down_weight, preferred_element_type=jn...  23.6 us
    dot_general x1, matrix products, local(): jnp.einsum('jmd,jdf->jmf', grouped, gate_weight, preferred_element_type=j...  12.3 us
    reduce_scatter x1, waiting for transfers between devices, local(): moe_cols = lax.psum_scatter(mixture, 'ffn', scatter_dimension=1, tiled=True)  10.9 us
    gather x2, local copies, waits for them, and re-layouts, local(): jnp.take(flat_pages, key_rows, axis=0).reshape(CMAX + fresh_len, QKD)  10.1 us
    unnamed x22, local copies, waits for them, and re-layouts  9.92 us
  transfers between devices with their start and end apart: 6, of which 6 were waited for; matrix products, arithmetic and copies ran while one was open for 8% of the time, Pallas kernels for 0%

commit v1 on v0

--- a/solution.py
+++ b/solution.py
@@ -128,7 +128,21 @@
     normed_cols = (
         hidden_wide * lax.rsqrt(mean_square + EPSILON) * gain_cols.astype(jnp.float32)
     ).astype(jnp.bfloat16)
-    normed_half = lax.all_gather(normed_cols, "exp", axis=0, tiled=True)
+    ways, here, turn = (lax.axis_size("exp"), lax.axis_index("exp"), normed_cols.shape[0])
+    lengths = [n * ways if d == 0 else n for d, n in enumerate(normed_cols.shape)]
+    full = lax.dynamic_update_slice_in_dim(
+        jnp.zeros(lengths, normed_cols.dtype), normed_cols, here * turn, axis=0
+    )
+    going_up = going_down = normed_cols
+    for far in range(1, ways // 2 + 1):
+        going_up = lax.ppermute(going_up, "exp", [(d, (d + 1) % ways) for d in range(ways)])
+        full = lax.dynamic_update_slice_in_dim(full, going_up, (here - far) % ways * turn, axis=0)
+        if 2 * far < ways:
+            going_down = lax.ppermute(going_down, "exp", [(d, (d - 1) % ways) for d in range(ways)])
+            full = lax.dynamic_update_slice_in_dim(
+                full, going_down, (here + far) % ways * turn, axis=0
+            )
+    normed_half = full
     normed_all = lax.all_gather(normed_half, "ffn", axis=1, tiled=True)
     expert_ids = lax.broadcasted_iota(jnp.int32, (1, 1, EXPERTS), 2)
     route_hot = routes_all[:, :, None] == expert_ids

time: 244 us -> 235 us (0.963)
  waiting for transfers between devices: 114 us -> 101 us
  starting transfers between devices: 0.42 us -> 4.26 us
    all_gather x1 -> x0, waiting for transfers between devices: 29.2 us -> none  [local(): normed_half = lax.all_gather(normed_cols, 'exp', axis=0, tiled=True)]
    ppermute x0 -> x3, waiting for transfers between devices: none -> 17.8 us  [the longest x2 13 us: local(): lax.ppermute(going_up, 'exp', [(d, (d + 1) % ways) for d in range(ways)])]
    ppermute x0 -> x3, starting transfers between devices: none -> 3.88 us  [the longest x1 2.1 us: local(): lax.ppermute(going_down, 'exp', [(d, (d - 1) % ways) for d in range(ways)])]
    unnamed x22 -> x24, local copies, waits for them, and re-layouts: 9.92 us -> 10.9 us
  transfers between devices with their start and end apart: 6 -> 8, of which waited for: 6 -> 7; matrix products, arithmetic and copies ran while one was open for 8% -> 8% of each run, Pallas kernels for 0% -> 0%
where the time goes in v1:
time: 235 us; the launch traced here: 234 us
  waiting for transfers between devices  101 us (43%)
  matrix products  54.4 us (23%)
  local copies, waits for them, and re-layouts  36.5 us (16%)
  other arithmetic  21.1 us (9%)
  between operations  14.2 us (6%)
  starting transfers between devices  4.26 us (2%)
  blocking collectives  2.47 us (1%)
    all_gather x1, waiting for transfers between devices, local(): gathered = lax.all_gather(share, ('exp', 'ffn'), axis=0, tiled=False)  35.9 us
    reduce_scatter x1, waiting for transfers between devices, local(): moe_out = lax.psum_scatter(moe_cols, 'exp', scatter_dimension=0, tiled=True)  31 us
    dot_general x1, matrix products, local(): jnp.einsum('jmf,jfd->jmd', active, down_weight, preferred_element_type=jn...  23.6 us
    ppermute x2, waiting for transfers between devices, local(): lax.ppermute(going_up, 'exp', [(d, (d + 1) % ways) for d in range(ways)])  13 us
    dot_general x1, matrix products, local(): jnp.einsum('jmd,jdf->jmf', grouped, gate_weight, preferred_element_type=j...  12.3 us
    unnamed x24, local copies, waits for them, and re-layouts  10.9 us
    gather x2, local copies, waits for them, and re-layouts, local(): jnp.take(flat_pages, key_rows, axis=0).reshape(CMAX + fresh_len, QKD)  10.1 us
    reduce_scatter x1, waiting for transfers between devices, local(): moe_cols = lax.psum_scatter(mixture, 'ffn', scatter_dimension=1, tiled=True)  9.91 us
  transfers between devices with their start and end apart: 8, of which 7 were waited for; matrix products, arithmetic and copies ran while one was open for 8% of the time, Pallas kernels for 0%

profile of v1, /device:TPU:0, one launch (start us, length us, event | category | flops | bytes accessed | tf_op | source)
XLA Modules:
  0.0 234.3 jit_solution(8121245977852328619)
XLA Ops:
  7.2 1.2 copy.43
  8.5 0.2 reshape.346
  8.7 0.7 convert_element_type.101
  9.4 0.1 copy.44
  9.5 0.2 convert_element_type.102
  9.8 0.1 dynamic-slice
  9.8 2.3 fusion.36
  12.3 0.1 concatenate.36
  12.4 0.1 add.237
  12.5 1.2 dynamic_slice.19
  13.7 1.2 dynamic_slice.20
  15.0 0.3 copy.45
  15.3 0.7 fusion.40
  16.0 0.1 compare_and_fusion
  16.1 0.1 broadcast_in_dim.83
  16.2 0.1 broadcast_in_dim.84
  16.3 1.3 copy.55
  17.5 0.7 fusion.70
  18.3 1.3 iota_compare_fusion.6
  19.6 1.0 and_or_fusion
  20.7 35.9 %all-gather.7.cloned.1.call-done = bf16[8,21,9216]{2,1,0:T(8,128)(2,1)} async-done(((bf16[1,21,9216]{2,1,0:T(8,128)(2,1)}), bf16[8,21,9216]{2,1,0:T(8,128)(2,1)}) %all-gather.7.cloned.1.call-update) | async-done | bytes 3096592 | tf_op jit(solution)/shard_map/all_gather | solution.py:69
  56.6 4.8 %reshape.369 = bf16[168,9216]{1,0:T(8,128)(2,1)} reshape(bf16[8,21,9216]{2,1,0:T(8,128)(2,1)} %all-gather.7.cloned.1.call-done) | data formatting | bytes 6193152
  61.4 6.3 %gather_fusion = bf16[80,9216]{1,0:T(8,128)(2,1)} fusion(bf16[168,9216]{1,0:T(8,128)(2,1)} %reshape.369, s32[1024]{0:T(1024)S(1)} %pad_clamp_fusion), kind=kCustom, calls=%fused_computation | custom fusion | bytes 2949440 | tf_op jit(solution)/shard_map/jit(_take)/gather | solution.py:92
  67.7 2.7 %broadcast_select_fusion = bf16[80,9216]{1,0:T(8,128)(2,1)} fusion(bf16[80,9216]{1,0:T(8,128)(2,1)} %gather_fusion, pred[80]{0:T(512)(128)(4,1)S(1)} %compare_and_fusion), kind=kLoop, calls=%fused_computation.21 | loop fusion | flops 737280 | bytes 2949200 | tf_op jit(solution)/shard_map/jit(_take)/select_n | solution.py:92
  70.3 3.9 %gather.7 = bf16[1280,576]{1,0:T(8,128)(2,1)} reshape(bf16[80,9216]{1,0:T(8,128)(2,1)} %gather_fusion) | data formatting | bytes 2949120 | tf_op jit(solution)/shard_map/jit(_take)/gather | solution.py:92
  74.2 3.9 %select_n.143 = bf16[1280,576]{1,0:T(8,128)(2,1)} reshape(bf16[80,9216]{1,0:T(8,128)(2,1)} %broadcast_select_fusion) | data formatting | bytes 2949120 | tf_op jit(solution)/shard_map/jit(_take)/select_n | solution.py:92
  78.1 2.6 %fusion.6 = f32[128,4,1280]{0,2,1:T(8,128)S(1)} fusion(bf16[128,4,576]{0,2,1:T(8,128)(2,1)S(1)} %bitcast.75, bf16[1280,576]{1,0:T(8,128)(2,1)} %select_n.143, pred[128,1280]{0,1:T(8,128)(4,1)S(1)} %and_or_fusion), kind=kOutput, calls=%fused_computation.13 | convolution fusion | flops 756285440 | bytes 4849664 | tf_op jit(solution)/shard_map/thd,kd->thk/dot_general | solution.py:97
  80.8 1.5 copy-done.4
  82.3 0.6 fusion.50
  82.9 4.4 %fusion.23 = bf16[4,128,128]{1,2,0:T(8,128)(2,1)S(1)} fusion(bf16[512,4,128]{0,2,1:T(8,128)(2,1)S(1)} %bitcast.76, bf16[1280,576]{1,0:T(8,128)(2,1)} %gather.7, pred[1280]{0:T(1024)(128)(4,1)S(1)} %broadcast_in_dim.84, f32[128,4]{0,1:T(4,128)S(1)} %fusion.50, f32[128,4,1280]{0,2,1:T(8,128)} %copy-done.4), kind=kOutput, calls=%fused_computation.32 | convolution fusion | flops 741148416 | bytes 7212288 | tf_op jit(solution)/shard_map/thl,lhd->thd/dot_general | solution.py:113
  87.3 1.3 convolution_convert_fusion.2
  88.5 0.2 all-gather.5.cloned.1.call-start
  88.8 6.7 %reduce-scatter.4.cloned.1.call-done = bf16[128,1024]{1,0:T(8,128)(2,1)} async-done(((bf16[128,2048]{1,0:T(8,128)(2,1)}), bf16[128,1024]{1,0:T(8,128)(2,1)}) %reduce-scatter.4.cloned.1.call-update) | async-done | bytes 262160 | tf_op jit(solution)/shard_map/reduce_scatter | solution.py:119
  95.5 1.1 fusion.30
  96.6 2.5 %psum.7 = f32[128,1]{0,1:T(1,128)S(1)} all-reduce(f32[128,1]{0,1:T(1,128)S(1)} %bitcast.79), channel_id=1, replica_groups=mesh['req'=4,'exp'=4,'ffn'=2] {'ffn'}, use_global_device_ids=true, to_apply=%region_7.8 | all-reduce | flops 128 | bytes 1024 | tf_op jit(solution)/shard_map/psum | solution.py:125
  99.1 0.1 broadcast_in_dim.88
  99.2 0.1 constant_dynamic-update-slice_fusion.3
  99.4 1.8 collective-permute-start
  101.1 2.1 collective-permute-start.1
  103.2 7.1 %collective-permute-done = bf16[128,1024]{1,0:T(8,128)(2,1)S(1)} collective-permute-done((bf16[128,1024]{1,0:T(8,128)(2,1)S(1)}, bf16[128,1024]{1,0:T(8,128)(2,1)S(1)}, u32[]{:S(2)}, u32[]{:S(2)}) %collective-permute-start) | collective-permute-done | bytes 262176 | tf_op jit(solution)/shard_map/ppermute | solution.py:138
  110.4 4.8 %collective-permute-done.1 = bf16[128,1024]{1,0:T(8,128)(2,1)S(1)} collective-permute-done((bf16[128,1024]{1,0:T(8,128)(2,1)S(1)}, bf16[128,1024]{1,0:T(8,128)(2,1)S(1)}, u32[]{:S(2)}, u32[]{:S(2)}) %collective-permute-start.1) | collective-permute-done | bytes 262176 | tf_op jit(solution)/shard_map/ppermute | solution.py:141
  115.2 5.9 %collective-permute-done.2 = bf16[128,1024]{1,0:T(8,128)(2,1)S(1)} collective-permute-done((bf16[128,1024]{1,0:T(8,128)(2,1)S(1)}, bf16[128,1024]{1,0:T(8,128)(2,1)S(1)}, u32[]{:S(2)}, u32[]{:S(2)}) %collective-permute-start.2) | collective-permute-done | bytes 262176 | tf_op jit(solution)/shard_map/ppermute | solution.py:138
  121.1 1.0 copy-done.3
  122.2 0.1 add.245
  122.3 4.7 %reshape.351 = bf16[4,42,9216]{2,1,0:T(8,128)(2,1)} reshape(bf16[8,21,9216]{2,1,0:T(8,128)(2,1)} %all-gather.7.cloned.1.call-done) | data formatting | bytes 6193152 | tf_op jit(solution)/shard_map/reshape | solution.py:70
  127.0 1.2 slice.15
  128.3 0.2 reshape.355
  128.5 0.1 copy.51
  128.6 0.3 fusion.22
  128.9 0.2 convert_element_type.117
  129.1 0.1 add_select_fusion
  129.3 0.1 copy.49
  129.4 2.3 fusion.2
  131.7 1.4 fusion.1
  133.1 2.3 fusion.52
  135.6 1.7 select_reduce_fusion
  137.3 3.9 %convolution_convert_fusion = bf16[1024,2048]{1,0:T(8,128)(2,1)S(1)} fusion(pred[1024,512]{1,0:T(8,128)(4,1)S(1)} %fusion.2, bf16[512,2048]{1,0:T(8,128)(2,1)} %all-gather.5.cloned.1.call-done), kind=kOutput, calls=%fused_computation.9 | convolution fusion | flops 2149580800 | bytes 6815744 | tf_op jit(solution)/shard_map/dot_general | solution.py:176
  141.2 2.0 copy-done.2
  143.2 12.3 %fusion.51 = f32[8,128,704]{1,2,0:T(8,128)} fusion(bf16[8,128,2048]{2,1,0:T(8,128)(2,1)S(1)} %bitcast.73, bf16[8,2048,704]{1,2,0:T(8,128)(2,1)} %param.27), kind=kOutput, calls=%fused_computation.93 | convolution fusion | flops 2952790016 | bytes 30146560 | tf_op jit(solution)/shard_map/jmd,jdf->jmf/dot_general | solution.py:178
  155.5 23.6 %fusion.8 = f32[8,128,2048]{2,1,0:T(8,128)} fusion(bf16[8,704,2048]{2,1,0:T(8,128)(2,1)} %param.29, f32[8,128,704]{1,2,0:T(8,128)} %fusion.51, bf16[8,128,2048]{2,1,0:T(8,128)(2,1)} %bitcast.74, bf16[8,2048,704]{1,2,0:T(8,128)(2,1)} %param.28), kind=kOutput, calls=%fused_computation.19 | convolution fusion | flops 5909905408 | bytes 61603840 | tf_op jit(solution)/shard_map/jmf,jfd->jmd/dot_general | solution.py:181
  179.1 3.9 %fusion.3 = bf16[1024,2048]{1,0:T(8,128)(2,1)S(1)} fusion(f32[8,128,2048]{2,1,0:T(8,128)} %fusion.8, f32[1024]{0:T(1024)S(1)} %select_reduce_fusion), kind=kLoop, calls=%fused_computation.8 | loop fusion | flops 4194304 | bytes 12587008 | tf_op jit(solution)/shard_map/convert_element_type | solution.py:182
  183.0 3.8 %convolution_convert_fusion.1 = bf16[512,2048]{1,0:T(8,128)(2,1)} fusion(pred[512,1024]{1,0:T(8,128)(4,1)S(1)} %fusion.1, bf16[1024,2048]{1,0:T(8,128)(2,1)S(1)} %fusion.3), kind=kOutput, calls=%fused_computation.15 | convolution fusion | flops 2148532224 | bytes 6815744 | tf_op jit(solution)/shard_map/dot_general | solution.py:185
  186.8 9.9 %reduce-scatter.6.cloned.1.call-done = bf16[512,1024]{1,0:T(8,128)(2,1)} async-done(((bf16[512,2048]{1,0:T(8,128)(2,1)}), bf16[512,1024]{1,0:T(8,128)(2,1)}) %reduce-scatter.6.cloned.1.call-update) | async-done | bytes 1048592 | tf_op jit(solution)/shard_map/reduce_scatter | solution.py:186
  196.7 31.0 %reduce-scatter.8.cloned.1.call-done = bf16[128,1024]{1,0:T(8,128)(2,1)} async-done(((bf16[512,1024]{1,0:T(8,128)(2,1)}), bf16[128,1024]{1,0:T(8,128)(2,1)}) %reduce-scatter.8.cloned.1.call-update) | async-done | bytes 262160 | tf_op jit(solution)/shard_map/reduce_scatter | solution.py:187
  (51 shorter events, 0.9 us)
Async XLA Ops:
  7.2 80.1 %copy-start = (bf16[512,2048]{1,0:T(8,128)(2,1)S(1)}, bf16[512,2048]{1,0:T(8,128)(2,1)}, u32[]{:S(2)}) copy-start(bf16[512,2048]{1,0:T(8,128)(2,1)} %param.24) | copy-start | bytes 6291460
  7.2 7.8 %copy-start.6 = (bf16[128,2304]{1,0:T(8,128)(2,1)S(1)}, bf16[128,2304]{1,0:T(8,128)(2,1)}, u32[]{:S(2)}) copy-start(bf16[128,2304]{1,0:T(8,128)(2,1)} %param.16) | copy-start | bytes 1769476
  7.2 49.4 %all-gather.7.cloned.1.call-start = ((), (), s32[]{:S(2)}) async-start(), calls=%async_computation.7 | async-start | bytes 3981312 | tf_op jit(solution)/shard_map/all_gather | solution.py:69
  12.2 83.3 %reduce-scatter.4.cloned.1.call-start = ((), (), s32[]{:S(2)}) async-start(), calls=%async_computation.3 | async-start | bytes 786432 | tf_op jit(solution)/shard_map/reduce_scatter | solution.py:119
  80.8 1.5 copy-start.4
  87.2 1.6 copy-start.9
  87.2 8.3 %copy-start.8 = (bf16[128,2048]{1,0:T(8,128)(2,1)S(1)}, bf16[128,2048]{1,0:T(8,128)(2,1)}, u32[]{:S(2)}) copy-start(bf16[128,2048]{1,0:T(8,128)(2,1)} %param.15) | copy-start | bytes 1572868
  88.5 44.6 %all-gather.5.cloned.1.call-start = ((), (), s32[]{:S(2)}) async-start(), calls=%async_computation.4 | async-start | bytes 3145728 | tf_op jit(solution)/shard_map/all_gather | solution.py:146
  96.6 30.3 %copy-start.5 = (bf16[128,1024]{1,0:T(8,128)(2,1)}, bf16[128,1024]{1,0:T(8,128)(2,1)S(1)}, u32[]{:S(2)}) copy-start(bf16[128,1024]{1,0:T(8,128)(2,1)S(1)} %get-tuple-element.5) | copy-start | bytes 786436
  99.4 11.0 %collective-permute-start = (bf16[128,1024]{1,0:T(8,128)(2,1)S(1)}, bf16[128,1024]{1,0:T(8,128)(2,1)S(1)}, u32[]{:S(2)}, u32[]{:S(2)}) collective-permute-start(bf16[128,1024]{1,0:T(8,128)(2,1)S(1)} %get-tuple-element.3), channel_id=1, source_target_pairs={{0,2},{2,4},{4,6},{6,0},{1,3},{3,5},{5,7},{7,1},{8,10},{10,12},{12... | collective-permute-start | bytes 786440 | tf_op jit(solution)/shard_map/ppermute | solution.py:138
  101.1 14.0 %collective-permute-start.1 = (bf16[128,1024]{1,0:T(8,128)(2,1)S(1)}, bf16[128,1024]{1,0:T(8,128)(2,1)S(1)}, u32[]{:S(2)}, u32[]{:S(2)}) collective-permute-start(bf16[128,1024]{1,0:T(8,128)(2,1)S(1)} %get-tuple-element.3), channel_id=1, source_target_pairs={{0,6},{2,0},{4,2},{6,4},{1,7},{3,1},{5,3},{7,5},{8,14},{10,8},{12,... | collective-permute-start | bytes 786440 | tf_op jit(solution)/shard_map/ppermute | solution.py:141
  110.4 10.7 %collective-permute-start.2 = (bf16[128,1024]{1,0:T(8,128)(2,1)S(1)}, bf16[128,1024]{1,0:T(8,128)(2,1)S(1)}, u32[]{:S(2)}, u32[]{:S(2)}) collective-permute-start(bf16[128,1024]{1,0:T(8,128)(2,1)S(1)} %collective-permute-done), channel_id=1, source_target_pairs={{0,2},{2,4},{4,6},{6,0},{1,3},{3,5},{5,7},{7,1},{8,10},{10,12},{12... | collective-permute-start | bytes 786440 | tf_op jit(solution)/shard_map/ppermute | solution.py:138
  121.1 1.0 copy-start.3
  122.1 74.6 %reduce-scatter.6.cloned.1.call-start = ((), (), s32[]{:S(2)}) async-start(), calls=%async_computation.5 | async-start | bytes 3145728 | tf_op jit(solution)/shard_map/reduce_scatter | solution.py:186
  127.0 6.1 %copy-start.7 = (bf16[2048,32]{0,1:T(8,128)(2,1)S(1)}, bf16[2048,32]{0,1:T(8,128)(2,1)}, u32[]{:S(2)}) copy-start(bf16[2048,32]{0,1:T(8,128)(2,1)} %param.26) | copy-start | bytes 393220
  141.2 2.0 copy-start.2
  183.0 44.8 %copy-start.1 = (bf16[512,2048]{1,0:T(8,128)(2,1)S(1)}, bf16[512,2048]{1,0:T(8,128)(2,1)}, u32[]{:S(2)}) copy-start(bf16[512,2048]{1,0:T(8,128)(2,1)} %param.24) | copy-start | bytes 6291460
  186.7 41.0 %reduce-scatter.8.cloned.1.call-start = ((), (), s32[]{:S(2)}) async-start(), calls=%async_computation.6 | async-start | bytes 1310720 | tf_op jit(solution)/shard_map/reduce_scatter | solution.py:187
Sparse Core Ops, SparseCore 0:
  12.3 44.2 all-gather.6
  88.7 6.7 reduce-scatter.3
  122.2 9.8 all-gather.4
  186.9 9.7 reduce-scatter.5
  199.4 28.3 reduce-scatter.7
